TPU v7x, 256 devices: a whole 4x4x8 slice. The times are simulated.
256 devices in a mesh: col: 64 (over x, z, core), row: 4 (over y).
Axes of the slice: x: 4, y: 4, z: 8, core: 2. Of those that a mesh axis runs over, the one named last changes fastest.
Arguments:
- matrix: float32 [16, 4, 256, 1, 64, 256], P(None, 'row', None, None, 'col'), as said below
Outputs:
- factored: float32 [16, 4, 256, 1, 64, 256], P(None, 'row', None, None, 'col')
Inputs may be any that keep to these rules, and one draw needn't show every extreme that they name: matrix is symmetric and positive definite, a Matern covariance of spatial sites plus a symmetric measurement term and a nugget.
All inputs are finite; a program needn't handle non-finite values.
Results may differ from a plain program's by a relative error of at most 0.0003.
Values sent between devices are 32-bit elements; how exact they have to be, the bound alone decides.
No kernel may reach another device: no remote copies, remote signals or barrier semaphores. Data moves between devices by JAX's collectives and lax.ppermute only.
A program may use at most 128 MiB of HBM per device.

v0:
```python
import jax
import jax.numpy as jnp
from jax import lax
from jax.sharding import PartitionSpec as P

STEPS = 3
HI = lax.Precision.HIGHEST


def mm_hi(a, b):
    return jnp.einsum(
        "...ps,qs->...pq", a, b, precision=HI, preferred_element_type=jnp.float32
    )


def mm_lo(a, b):
    return jnp.einsum(
        "...ps,qs->...pq",
        a.astype(jnp.bfloat16),
        b.astype(jnp.bfloat16),
        preferred_element_type=jnp.float32,
    )


def factor(tile, eye):
    half = tile.shape[0] // 2
    unit = eye[:half, :half]
    la = jnp.linalg.cholesky(tile[:half, :half])
    ia = lax.linalg.triangular_solve(la, unit, left_side=True, lower=True)
    lb = mm_hi(tile[half:, :half], ia)
    lc = jnp.linalg.cholesky(tile[half:, half:] - mm_hi(lb, lb))
    ic = lax.linalg.triangular_solve(lc, unit, left_side=True, lower=True)
    corner = -jnp.matmul(ic, jnp.matmul(lb, ia, precision=HI), precision=HI)
    zero = jnp.zeros_like(unit)
    low = jnp.block([[la, zero], [lb, lc]])
    inverse = jnp.block([[ia, zero], [corner, ic]])
    return low, inverse


def on_device(matrix):
    tile_rows = matrix.shape[0]
    width = matrix.shape[2]
    n_row = lax.axis_size("row")
    n_col = lax.axis_size("col")
    quarter = width // n_row
    my_row = lax.axis_index("row")
    my_col = lax.axis_index("col")
    tiles = matrix.reshape(tile_rows, width, width)
    eye = jnp.eye(width, dtype=jnp.float32)

    head = lax.all_gather(tiles[0], "row", axis=0, tiled=False)

    cols = lax.dynamic_slice_in_dim(head[:STEPS], my_row * quarter, quarter, axis=2)
    piece = jnp.swapaxes(cols, 1, 2)
    perm = []
    for c in range(n_col):
        for r in range(n_row):
            dst_col = c - c % n_row + r
            perm.append((c * n_row + r, dst_col * n_row + c % n_row))
    piece = lax.ppermute(piece, ("col", "row"), perm)

    gathered = lax.all_gather(piece, "col", axis=1, tiled=False)
    raw = gathered.reshape(STEPS, tile_rows, width, width)

    pick = jnp.stack(
        [
            lax.dynamic_index_in_dim(raw[:, 0], my_row % STEPS, 0, keepdims=False),
            lax.dynamic_index_in_dim(raw[:, 0], (my_row + 1) % STEPS, 0, keepdims=False),
        ]
    )
    lead = lax.all_gather(pick, "row", axis=0, tiled=False)
    a00 = lead[0, 0]
    a10 = lead[0, 1].T
    a11 = lead[1, 0]
    a21 = lead[1, 1].T
    a22 = lead[2, 0]
    a20 = lead[2, 1]

    l0, i0 = factor(a00, eye)
    p01 = mm_hi(a10, i0)
    p02 = mm_hi(a20, i0)
    b11 = a11 - mm_hi(p01, p01)
    b21 = a21 - mm_hi(p02, p01)
    b22 = a22 - mm_hi(p02, p02)
    l1, i1 = factor(b11, eye)
    p12 = mm_hi(b21, i1)
    c22 = b22 - mm_hi(p12, p12)
    l2, i2 = factor(c22, eye)

    def sub(step, target, low_rows, partner, exact_rows):
        lo = mm_lo(low_rows, partner)
        hi = mm_hi(exact_rows, partner)
        t0 = my_row
        exact = (t0 == step) | (t0 == step + 1)
        first = jnp.where(exact, hi, lo[0])
        return target - lo.at[0].set(first)

    q0 = mm_hi(raw[0], i0)
    m1 = sub(1, raw[1], q0, p01, q0[0])
    q1 = mm_hi(m1, i1)
    m2 = sub(2, raw[2], q0, p02, q0[0])
    m2 = sub(2, m2, q1, p12, q1[0])
    q2 = mm_hi(m2, i2)

    own = jnp.swapaxes(head[:STEPS], 1, 2)
    c = my_col

    def own_sub(step, target, rows, partner):
        exact = (c == step) | (c == step + 1)
        return target - jnp.where(exact, mm_hi(rows, partner), mm_lo(rows, partner))

    r0 = mm_hi(own[0], i0)
    r1 = mm_hi(own_sub(1, own[1], r0, p01), i1)
    r2 = mm_hi(own_sub(2, own_sub(2, own[2], r0, p02), r1, p12), i2)

    update = mm_lo(q0, r0) + mm_lo(q1, r1) + mm_lo(q2, r2)
    offset = (my_row - c) % n_row
    near = c + offset
    local = jnp.clip((near - my_row) // n_row, 0, tile_rows - 1)
    valid = (offset <= 1) & (near < tile_rows * n_row)

    def row_of(q):
        return lax.dynamic_index_in_dim(q, local, 0, keepdims=False)

    exact = mm_hi(row_of(q0), r0) + mm_hi(row_of(q1), r1) + mm_hi(row_of(q2), r2)
    before = lax.dynamic_index_in_dim(update, local, 0, keepdims=False)
    chosen = jnp.where(valid, exact, before)
    update = lax.dynamic_update_index_in_dim(update, chosen, local, 0)

    row_ids = (jnp.arange(tile_rows, dtype=jnp.int32) * n_row + my_row)[:, None, None]
    trailing = jnp.where(row_ids >= c, tiles - update, tiles)
    panel = jnp.where(c == 0, q0, jnp.where(c == 1, q1, q2))
    diag = jnp.where(c == 0, l0, jnp.where(c == 1, l1, l2))
    leading = jnp.where(row_ids > c, panel, jnp.where(row_ids == c, diag[None], tiles))
    out = jnp.where(c >= STEPS, trailing, leading)
    return out.reshape(matrix.shape)


def solution(mesh):
    placed = (P(None, "row", None, None, "col", None),)
    return jax.shard_map(
        on_device,
        mesh=mesh,
        in_specs=placed,
        out_specs=P(None, "row", None, None, "col", None),
        check_vma=False,
    )
```

profile of v0, /device:TPU:16, one launch (start us, length us, event | category | flops | bytes accessed | tf_op | source)
XLA Modules:
  0.0 406.9 jit_solution(16917355489168281022)
XLA Ops:
  8.5 29.2 %all-gather.7.cloned.1.call-done = f32[4,1,256,1,1,256]{5,2,4,3,1,0:T(8,128)} async-done(((f32[1,1,256,1,1,256]{5,2,4,3,1,0:T(8,128)}), f32[4,1,256,1,1,256]{5,2,4,3,1,0:T(8,128)}) %all-gather.7.cloned.1.call-update) | async-done | bytes 1048592 | tf_op jit(solution)/shard_map/all_gather | solution.py:51
  39.2 4.4 %collective-permute-start = (f32[3,64,256]{2,1,0:T(8,128)S(1)}, f32[3,64,256]{2,1,0:T(8,128)S(1)}, u32[]{:S(2)}, u32[]{:S(2)}) collective-permute-start(f32[3,64,256]{2,1,0:T(8,128)S(1)} %dynamic-slice_bitcast_fusion.2), channel_id=1, source_target_pairs={{0,0},{1,4},{2,8},{3,12},{4,1},{5,5},{6,9},{7,13},{8,2},{9,6},{10,... | collective-permute-start | bytes 589832 | tf_op jit(solution)/shard_map/ppermute | solution.py:60
  43.6 6.6 %collective-permute-done = f32[3,64,256]{2,1,0:T(8,128)S(1)} collective-permute-done((f32[3,64,256]{2,1,0:T(8,128)S(1)}, f32[3,64,256]{2,1,0:T(8,128)S(1)}, u32[]{:S(2)}, u32[]{:S(2)}) %collective-permute-start) | collective-permute-done | bytes 196640 | tf_op jit(solution)/shard_map/ppermute | solution.py:60
  51.0 90.8 %all-gather.9.cloned.1.call-done = f32[3,4096,256]{2,1,0:T(8,128)} async-done(((f32[3,64,256]{2,1,0:T(8,128)}), f32[3,4096,256]{2,1,0:T(8,128)}) %all-gather.9.cloned.1.call-update) | async-done | bytes 12582928 | tf_op jit(solution)/shard_map/all_gather | solution.py:62
  144.0 9.5 %fusion.140 = (f32[1,4096,256]{2,1,0:T(8,128)}, f32[1,4096,256]{2,1,0:T(8,128)}, f32[1,4096,256]{2,1,0:T(8,128)}) fusion(f32[3,4096,256]{2,1,0:T(8,128)} %all-gather.9.cloned.1.call-done), kind=kLoop, calls=%fused_computation.222 | loop fusion | bytes 25165824 | tf_op jit(solution)/shard_map/slice | solution.py:101
  153.5 19.6 %all-gather.11.cloned.1.call-done = f32[8,256,256]{2,1,0:T(8,128)} async-done(((f32[2,256,256]{2,1,0:T(8,128)}), f32[8,256,256]{2,1,0:T(8,128)}) %all-gather.11.cloned.1.call-update) | async-done | bytes 2097168 | tf_op jit(solution)/shard_map/all_gather | solution.py:71
  173.0 2.1 copy.52
  175.3 11.7 %cholesky.104 = f32[128,128]{1,0:T(8,128)S(1)} custom-call(f32[128,128]{1,0:T(8,128)S(1)} %fusion.87), custom_call_target="Cholesky" | custom-call | tf_op jit(solution)/shard_map/jit(cholesky)/cholesky | solution.py:28
  189.0 9.8 %custom-call.10 = f32[1,128,128]{1,2,0:T(8,128)S(1)} custom-call(f32[1,128,128]{2,1,0:T(8,128)S(1)} %get-tuple-element.53), custom_call_target="InvertDiagBlocksLowerTriangular" | custom-call | tf_op jit(solution)/shard_map/triangular_solve/custom-call.0 | solution.py:29
  200.3 11.7 %cholesky.115 = f32[128,128]{1,0:T(8,128)S(1)} custom-call(f32[128,128]{1,0:T(8,128)S(1)} %fusion.85), custom_call_target="Cholesky" | custom-call | tf_op jit(solution)/shard_map/jit(cholesky)/cholesky | solution.py:31
  214.1 10.0 %custom-call.11 = f32[1,128,128]{1,2,0:T(8,128)S(1)} custom-call(f32[1,128,128]{2,1,0:T(8,128)S(1)} %get-tuple-element.51), custom_call_target="InvertDiagBlocksLowerTriangular" | custom-call | tf_op jit(solution)/shard_map/triangular_solve/custom-call.0 | solution.py:32
  230.6 13.2 %cholesky.126 = f32[128,128]{1,0:T(8,128)} custom-call(f32[128,128]{1,0:T(8,128)} %fusion.83), custom_call_target="Cholesky" | custom-call | tf_op jit(solution)/shard_map/jit(cholesky)/cholesky | solution.py:28
  245.3 2.1 select_bitcast_fusion.3
  247.3 11.3 %custom-call.12 = f32[1,128,128]{1,2,0:T(8,128)} custom-call(f32[1,128,128]{2,1,0:T(8,128)} %get-tuple-element.49), custom_call_target="InvertDiagBlocksLowerTriangular" | custom-call | tf_op jit(solution)/shard_map/triangular_solve/custom-call.0 | solution.py:29
  261.7 1.8 convolution_subtract_fusion.5
  267.6 12.2 %cholesky.137 = f32[128,128]{1,0:T(8,128)S(1)} custom-call(f32[128,128]{1,0:T(8,128)S(1)} %fusion.81), custom_call_target="Cholesky" | custom-call | tf_op jit(solution)/shard_map/jit(cholesky)/cholesky | solution.py:31
  281.1 9.8 %custom-call.13 = f32[1,128,128]{1,2,0:T(8,128)S(1)} custom-call(f32[1,128,128]{2,1,0:T(8,128)S(1)} %get-tuple-element.47), custom_call_target="InvertDiagBlocksLowerTriangular" | custom-call | tf_op jit(solution)/shard_map/triangular_solve/custom-call.0 | solution.py:32
  295.3 11.7 %cholesky.148 = f32[128,128]{1,0:T(8,128)S(1)} custom-call(f32[128,128]{1,0:T(8,128)S(1)} %fusion.79), custom_call_target="Cholesky" | custom-call | tf_op jit(solution)/shard_map/jit(cholesky)/cholesky | solution.py:28
  308.8 9.8 %custom-call.14 = f32[1,128,128]{1,2,0:T(8,128)S(1)} custom-call(f32[1,128,128]{2,1,0:T(8,128)S(1)} %get-tuple-element.45), custom_call_target="InvertDiagBlocksLowerTriangular" | custom-call | tf_op jit(solution)/shard_map/triangular_solve/custom-call.0 | solution.py:29
  323.7 5.3 %fusion.36 = f32[16,256,256]{2,1,0:T(8,128)S(1)} fusion(f32[16,256,256]{2,1,0:T(8,128)} %bitcast.225, f32[128,128]{1,0:T(8,128)S(1)} %fusion.51, f32[128,128]{1,0:T(8,128)S(1)} %copy-done.9, f32[128,128]{1,0:T(8,128)S(1)} %copy-done.11), kind=kOutput, calls=%fused_computation.79 | convolution fusion | flops 3221487616 | bytes 8585216 | tf_op jit(solution)/shard_map/...ps,qs->...pq/dot_general | solution.py:11
  329.0 3.1 fusion.60
  335.1 3.5 fusion.6
  338.6 3.2 fusion.21
  342.0 2.7 fusion.23
  344.7 2.7 fusion.65
  347.4 11.7 %cholesky.159 = f32[128,128]{1,0:T(8,128)S(1)} custom-call(f32[128,128]{1,0:T(8,128)S(1)} %fusion.77), custom_call_target="Cholesky" | custom-call | tf_op jit(solution)/shard_map/jit(cholesky)/cholesky | solution.py:31
  360.5 10.0 %custom-call.15 = f32[1,128,128]{1,2,0:T(8,128)S(1)} custom-call(f32[1,128,128]{2,1,0:T(8,128)S(1)} %get-tuple-element.43), custom_call_target="InvertDiagBlocksLowerTriangular" | custom-call | tf_op jit(solution)/shard_map/triangular_solve/custom-call.0 | solution.py:32
  373.1 2.1 fusion.17
  375.2 2.2 fusion.15
  379.7 6.4 %fusion.3 = f32[16,256,256]{2,1,0:T(8,128)S(1)} fusion(f32[16,256,256]{2,1,0:T(8,128)} %fusion.15, f32[16,256,256]{2,1,0:T(8,128)} %bitcast.226, f32[16,256,256]{2,1,0:T(8,128)S(1)} %copy-done.4, f32[128,128]{1,0:T(8,128)S(1)} %fusion.43, f32[128,128]{1,0:T(8,128)S(1)} %copy.70, f32[128,128]{1,0:T(8,128)S(1)} %convolution_negate_fusion), kind=kOutput, calls=%fused_computation.5 | convolution fusion | flops 3223584768 | bytes 16973824 | tf_op jit(solution)/shard_map/...ps,qs->...pq/dot_general | solution.py:11
  389.7 4.0 fusion.1
  393.7 6.3 %copy.74 = f32[16,1,256,1,1,256]{5,4,3,2,1,0:T(1,128)} copy(f32[16,1,256,1,1,256]{5,2,0,4,3,1:T(8,128)S(1)} %fusion.1) | data formatting | bytes 8388608 | tf_op jit(solution)/shard_map/reshape | solution.py:136
  (149 shorter events, 52.2 us)
Async XLA Ops:
  6.5 31.2 %all-gather.7.cloned.1.call-start = ((), (), s32[]{:S(2)}) async-start(), calls=%async_computation | async-start | bytes 1310720 | tf_op jit(solution)/shard_map/all_gather | solution.py:51
  8.4 133.3 %all-gather.9.cloned.1.call-start = ((), (), s32[]{:S(2)}) async-start(), calls=%async_computation.1 | async-start | bytes 12779520 | tf_op jit(solution)/shard_map/all_gather | solution.py:62
  39.2 11.0 %collective-permute-start = (f32[3,64,256]{2,1,0:T(8,128)S(1)}, f32[3,64,256]{2,1,0:T(8,128)S(1)}, u32[]{:S(2)}, u32[]{:S(2)}) collective-permute-start(f32[3,64,256]{2,1,0:T(8,128)S(1)} %dynamic-slice_bitcast_fusion.2), channel_id=1, source_target_pairs={{0,0},{1,4},{2,8},{3,12},{4,1},{5,5},{6,9},{7,13},{8,2},{9,6},{10,... | collective-permute-start | bytes 589832 | tf_op jit(solution)/shard_map/ppermute | solution.py:60
  50.2 0.7 copy-start.24
  50.9 122.2 %all-gather.11.cloned.1.call-start = ((), (), s32[]{:S(2)}) async-start(), calls=%async_computation.2 | async-start | bytes 2621440 | tf_op jit(solution)/shard_map/all_gather | solution.py:71
  199.3 0.6 copy-start.12
  224.5 22.9 %copy-start.8 = (f32[128,128]{1,0:T(8,128)}, f32[128,128]{1,0:T(8,128)S(1)}, u32[]{:S(2)}) copy-start(f32[128,128]{1,0:T(8,128)S(1)} %copy.57) | copy-start | bytes 196612
  224.8 0.6 copy-start.10
  226.2 0.7 copy-start.16
  260.8 3.8 copy-start.14
  265.7 54.4 %copy-start.15 = (f32[128,128]{0,1:T(8,128)S(1)}, f32[128,128]{0,1:T(8,128)}, u32[]{:S(2)}) copy-start(f32[128,128]{0,1:T(8,128)} %copy-done.14) | copy-start | bytes 196612
  265.7 55.2 %copy-start.13 = (f32[128,128]{0,1:T(8,128)S(1)}, f32[128,128]{0,1:T(8,128)}, u32[]{:S(2)}) copy-start(f32[128,128]{0,1:T(8,128)} %copy-done.12) | copy-start | bytes 196612
  265.7 55.9 %copy-start.9 = (f32[128,128]{1,0:T(8,128)S(1)}, f32[128,128]{1,0:T(8,128)}, u32[]{:S(2)}) copy-start(f32[128,128]{1,0:T(8,128)} %copy-done.8) | copy-start | bytes 196612
  265.7 55.9 %copy-start.11 = (f32[128,128]{1,0:T(8,128)S(1)}, f32[128,128]{1,0:T(8,128)}, u32[]{:S(2)}) copy-start(f32[128,128]{1,0:T(8,128)} %copy-done.10) | copy-start | bytes 196612
  329.0 15.6 %copy-start = (f32[16,256,256]{2,1,0:T(8,128)}, f32[16,256,256]{2,1,0:T(8,128)S(1)}, u32[]{:S(2)}) copy-start(f32[16,256,256]{2,1,0:T(8,128)S(1)} %fusion.36) | copy-start | bytes 12582916
  332.9 2.2 copy-start.5
  338.6 3.4 copy-start.2
  375.2 4.5 %copy-start.4 = (f32[16,256,256]{2,1,0:T(8,128)S(1)}, f32[16,256,256]{2,1,0:T(8,128)}, u32[]{:S(2)}) copy-start(f32[16,256,256]{2,1,0:T(8,128)} %fusion.17) | copy-start | bytes 12582916
  379.6 6.5 %copy-start.6 = (f32[16,256,256]{2,1,0:T(8,128)S(1)}, f32[16,256,256]{2,1,0:T(8,128)}, u32[]{:S(2)}) copy-start(f32[16,256,256]{2,1,0:T(8,128)} %fusion.23) | copy-start | bytes 12582916
  379.6 6.5 %copy-start.7 = (f32[16,256,256]{2,1,0:T(8,128)S(1)}, f32[16,256,256]{2,1,0:T(8,128)}, u32[]{:S(2)}) copy-start(f32[16,256,256]{2,1,0:T(8,128)} %fusion.65) | copy-start | bytes 12582916
  386.1 2.2 copy-start.3
  386.1 3.0 copy-start.17
  386.1 3.0 copy-start.18
  386.1 3.0 copy-start.19
  386.2 3.0 copy-start.20
  386.2 3.0 copy-start.21
  386.2 3.0 copy-start.22
  386.2 3.0 copy-start.23
  386.2 3.5 copy-start.1
Sparse Core Ops, SparseCore 0:
  9.1 28.5 all-gather.6
  51.0 90.7 all-gather.8
  144.0 29.0 all-gather.10
where the time goes:
time: 412 us; the launch traced here: 407 us
  other arithmetic  152 us (37%)
  waiting for transfers between devices  146 us (35%)
  matrix products  54.8 us (13%)
  local copies, waits for them, and re-layouts  34.8 us (8%)
  between operations  14.3 us (3%)
  starting transfers between devices  4.44 us (1%)
    all_gather x1, waiting for transfers between devices, on_device(): gathered = lax.all_gather(piece, 'col', axis=1, tiled=False)  90.8 us
    another operation x9, other arithmetic, factor(): la = jnp.linalg.cholesky(tile[:half, :half])  39.5 us
    another operation x9, other arithmetic, factor(): lc = jnp.linalg.cholesky(tile[half:, half:] - mm_hi(lb, lb))  37.8 us
    another operation x6, other arithmetic, factor(): ia = lax.linalg.triangular_solve(la, unit, left_side=True, lower=True)  35.4 us
    dot_general x28, matrix products, mm_hi(): jnp.einsum('...ps,qs->...pq', a, b, precision=HI, preferred_element_type=...  35.2 us
    another operation x6, other arithmetic, factor(): ic = lax.linalg.triangular_solve(lc, unit, left_side=True, lower=True)  32.4 us
    all_gather x1, waiting for transfers between devices, on_device(): head = lax.all_gather(tiles[0], 'row', axis=0, tiled=False)  29.2 us
    all_gather x1, waiting for transfers between devices, on_device(): lead = lax.all_gather(pick, 'row', axis=0, tiled=False)  19.6 us
  transfers between devices with their start and end apart: 4, of which 4 were waited for; matrix products, arithmetic and copies ran while one was open for 2% of the time, Pallas kernels for 0%

commit v1 on v0

--- a/solution.py
+++ b/solution.py
@@ -50,6 +50,12 @@
 
     head = lax.all_gather(tiles[0], "row", axis=0, tiled=False)
 
+    chunk = STEPS * width * width // n_col
+    chunks = lax.all_to_all(
+        head[:STEPS].reshape(n_col, chunk), "col", 0, 0, tiled=True
+    )
+    lead = lax.all_gather(chunks[:STEPS], "col", axis=0, tiled=False)
+
     cols = lax.dynamic_slice_in_dim(head[:STEPS], my_row * quarter, quarter, axis=2)
     piece = jnp.swapaxes(cols, 1, 2)
     perm = []
@@ -57,24 +63,19 @@
         for r in range(n_row):
             dst_col = c - c % n_row + r
             perm.append((c * n_row + r, dst_col * n_row + c % n_row))
+    piece, lead = lax.optimization_barrier((piece, lead))
     piece = lax.ppermute(piece, ("col", "row"), perm)
 
     gathered = lax.all_gather(piece, "col", axis=1, tiled=False)
     raw = gathered.reshape(STEPS, tile_rows, width, width)
 
-    pick = jnp.stack(
-        [
-            lax.dynamic_index_in_dim(raw[:, 0], my_row % STEPS, 0, keepdims=False),
-            lax.dynamic_index_in_dim(raw[:, 0], (my_row + 1) % STEPS, 0, keepdims=False),
-        ]
-    )
-    lead = lax.all_gather(pick, "row", axis=0, tiled=False)
-    a00 = lead[0, 0]
-    a10 = lead[0, 1].T
-    a11 = lead[1, 0]
-    a21 = lead[1, 1].T
-    a22 = lead[2, 0]
-    a20 = lead[2, 1]
+    block = [lead[:, j].reshape(STEPS, width, width) for j in range(STEPS)]
+    a00 = block[0][0]
+    a10 = block[0][1]
+    a20 = block[0][2]
+    a11 = block[1][1]
+    a21 = block[1][2]
+    a22 = block[2][2]
 
     l0, i0 = factor(a00, eye)
     p01 = mm_hi(a10, i0)

time: 412 us -> 406 us (0.985)
  waiting for transfers between devices: 146 us -> 112 us
  blocking collectives: 0 us -> 33.1 us
  matrix products: 54.8 us -> 34.9 us
  other arithmetic: 152 us -> 162 us
    all_gather x1, waiting for transfers between devices: 90.8 us -> 0.02 us  [on_device(): gathered = lax.all_gather(piece, 'col', axis=1, tiled=False)]
    all_gather x1, waiting for transfers between devices: 19.6 us -> 74.5 us  [on_device(): lead = lax.all_gather(chunks[:STEPS], 'col', axis=0, tiled=False)]
    all_to_all x0 -> x1, blocking collectives: none -> 33.1 us  [on_device(): lax.all_to_all(head[:STEPS].reshape(n_col, chunk), 'col', 0, 0, tiled=True)]
    dot_general x28, matrix products: 35.2 us -> 26.1 us  [mm_hi(): jnp.einsum('...ps,qs->...pq', a, b, precision=HI, preferred_element_type=...]
    another operation x6, other arithmetic: 32.4 us -> 41.3 us  [factor(): ic = lax.linalg.triangular_solve(lc, unit, left_side=True, lower=True)]
    all_gather x0 -> x1, other arithmetic: none -> 8.68 us  [on_device(): lead = lax.all_gather(chunks[:STEPS], 'col', axis=0, tiled=False)]
    dot_general x9, matrix products: 13.9 us -> 5.42 us  [mm_lo(): jnp.einsum('...ps,qs->...pq', a.astype(jnp.bfloat16), b.astype(jnp.bfloat...]
    slice x1 -> x5, local copies, waits for them, and re-layouts: 1.18 us -> 9.39 us  [the longest x1 7.72 us: on_device(): block = [lead[:, j].reshape(STEPS, width, width) for j in range(STEPS)]]
  transfers between devices with their start and end apart: 4 -> 4, of which waited for: 4 -> 3; matrix products, arithmetic and copies ran while one was open for 2% -> 45% of each run, Pallas kernels for 0% -> 0%
where the time goes in v1:
time: 406 us; the launch traced here: 399 us
  other arithmetic  162 us (40%)
  waiting for transfers between devices  112 us (28%)
  local copies, waits for them, and re-layouts  38.9 us (10%)
  matrix products  34.9 us (9%)
  blocking collectives  33.1 us (8%)
  between operations  14.4 us (4%)
    all_gather x1, waiting for transfers between devices, on_device(): lead = lax.all_gather(chunks[:STEPS], 'col', axis=0, tiled=False)  74.5 us
    another operation x6, other arithmetic, factor(): ic = lax.linalg.triangular_solve(lc, unit, left_side=True, lower=True)  41.3 us
    another operation x9, other arithmetic, factor(): lc = jnp.linalg.cholesky(tile[half:, half:] - mm_hi(lb, lb))  37.6 us
    another operation x9, other arithmetic, factor(): la = jnp.linalg.cholesky(tile[:half, :half])  37.3 us
    all_to_all x1, blocking collectives, on_device(): lax.all_to_all(head[:STEPS].reshape(n_col, chunk), 'col', 0, 0, tiled=True)  33.1 us
    another operation x6, other arithmetic, factor(): ia = lax.linalg.triangular_solve(la, unit, left_side=True, lower=True)  32.8 us
    all_gather x1, waiting for transfers between devices, on_device(): head = lax.all_gather(tiles[0], 'row', axis=0, tiled=False)  29.2 us
    dot_general x28, matrix products, mm_hi(): jnp.einsum('...ps,qs->...pq', a, b, precision=HI, preferred_element_type=...  26.1 us
  transfers between devices with their start and end apart: 4, of which 3 were waited for; matrix products, arithmetic and copies ran while one was open for 45% of the time, Pallas kernels for 0%

profile of v1, /device:TPU:16, one launch (start us, length us, event | category | flops | bytes accessed | tf_op | source)
XLA Modules:
  0.0 398.8 jit_solution(8184092143023780564)
XLA Ops:
  8.5 29.2 %all-gather.7.cloned.1.call-done = f32[4,1,256,1,1,256]{5,2,4,3,1,0:T(8,128)} async-done(((f32[1,1,256,1,1,256]{5,2,4,3,1,0:T(8,128)}), f32[4,1,256,1,1,256]{5,2,4,3,1,0:T(8,128)}) %all-gather.7.cloned.1.call-update) | async-done | bytes 1048592 | tf_op jit(solution)/shard_map/all_gather | solution.py:51
  39.7 33.1 %all_to_all.10 = f32[64,1,3072]{2,1,0:T(1,128)S(1)} all-to-all(f32[64,1,3072]{2,1,0:T(1,128)S(1)} %reshape.234), channel_id=1, replica_groups=mesh['col'=64,'row'=4] {'col'}, dimensions={0} | all-to-all | bytes 1572864 | tf_op jit(solution)/shard_map/all_to_all | solution.py:54
  73.8 74.5 %all-gather.9.cloned.1.call-done = f32[192,1,3072]{2,1,0:T(1,128)} async-done(((f32[3,1,3072]{2,1,0:T(1,128)}), f32[192,1,3072]{2,1,0:T(1,128)}) %all-gather.9.cloned.1.call-update) | async-done | bytes 2359312 | tf_op jit(solution)/shard_map/all_gather | solution.py:57
  148.3 8.7 %reduce.10 = f32[192,3072]{1,0:T(8,128)} reduce(f32[192,1,3072]{2,1,0:T(1,128)} %all-gather.9.cloned.1.call-done, f32[]{:T(128)} %constant.172), dimensions={1}, to_apply=%all-gather.1.reduce_sub_computation | reduce | bytes 4718596 | tf_op jit(solution)/shard_map/all_gather | solution.py:57
  157.0 3.0 reshape.197
  159.9 2.8 collective-permute-start
  162.7 8.4 %collective-permute-done = f32[3,64,256]{2,1,0:T(8,128)S(1)} collective-permute-done((f32[3,64,256]{2,1,0:T(8,128)S(1)}, f32[3,64,256]{2,1,0:T(8,128)S(1)}, u32[]{:S(2)}, u32[]{:S(2)}) %collective-permute-start) | collective-permute-done | bytes 196640 | tf_op jit(solution)/shard_map/ppermute | solution.py:67
  172.0 7.7 %slice_reduce_fusion = (f32[64,3072]{1,0:T(8,128)}, f32[64,3072]{1,0:T(8,128)}, f32[64,3072]{1,0:T(8,128)}) fusion(f32[64,3,3072]{2,1,0:T(4,128)S(1)} %reshape.197), kind=kLoop, calls=%fused_computation.46 | loop fusion | bytes 4718592 | tf_op jit(solution)/shard_map/slice | solution.py:72
  179.7 1.5 reshape_squeeze.9
  181.5 11.7 %cholesky.104 = f32[128,128]{1,0:T(8,128)S(1)} custom-call(f32[128,128]{1,0:T(8,128)S(1)} %fusion.87), custom_call_target="Cholesky" | custom-call | tf_op jit(solution)/shard_map/jit(cholesky)/cholesky | solution.py:28
  193.9 1.3 select_bitcast_fusion.5
  195.2 9.8 %custom-call.10 = f32[1,128,128]{1,2,0:T(8,128)S(1)} custom-call(f32[1,128,128]{2,1,0:T(8,128)S(1)} %get-tuple-element.60), custom_call_target="InvertDiagBlocksLowerTriangular" | custom-call | tf_op jit(solution)/shard_map/triangular_solve/custom-call.0 | solution.py:29
  206.6 11.7 %cholesky.115 = f32[128,128]{1,0:T(8,128)S(1)} custom-call(f32[128,128]{1,0:T(8,128)S(1)} %fusion.85), custom_call_target="Cholesky" | custom-call | tf_op jit(solution)/shard_map/jit(cholesky)/cholesky | solution.py:31
  219.0 1.2 select_bitcast_fusion.4
  220.2 18.5 %custom-call.11 = f32[1,128,128]{1,2,0:T(8,128)S(1)} custom-call(f32[1,128,128]{2,1,0:T(8,128)S(1)} %get-tuple-element.58), custom_call_target="InvertDiagBlocksLowerTriangular" | custom-call | tf_op jit(solution)/shard_map/triangular_solve/custom-call.0 | solution.py:32
  244.0 11.7 %cholesky.126 = f32[128,128]{1,0:T(8,128)S(1)} custom-call(f32[128,128]{1,0:T(8,128)S(1)} %fusion.83), custom_call_target="Cholesky" | custom-call | tf_op jit(solution)/shard_map/jit(cholesky)/cholesky | solution.py:28
  256.5 1.3 select_bitcast_fusion.3
  257.8 9.8 %custom-call.12 = f32[1,128,128]{1,2,0:T(8,128)S(1)} custom-call(f32[1,128,128]{2,1,0:T(8,128)S(1)} %get-tuple-element.56), custom_call_target="InvertDiagBlocksLowerTriangular" | custom-call | tf_op jit(solution)/shard_map/triangular_solve/custom-call.0 | solution.py:29
  269.2 12.1 %cholesky.137 = f32[128,128]{1,0:T(8,128)S(1)} custom-call(f32[128,128]{1,0:T(8,128)S(1)} %fusion.81), custom_call_target="Cholesky" | custom-call | tf_op jit(solution)/shard_map/jit(cholesky)/cholesky | solution.py:31
  282.0 1.3 select_bitcast_fusion.2
  283.3 9.8 %custom-call.13 = f32[1,128,128]{1,2,0:T(8,128)S(1)} custom-call(f32[1,128,128]{2,1,0:T(8,128)S(1)} %get-tuple-element.54), custom_call_target="InvertDiagBlocksLowerTriangular" | custom-call | tf_op jit(solution)/shard_map/triangular_solve/custom-call.0 | solution.py:32
  295.3 1.4 convolution_subtract_fusion.1
  297.3 11.7 %cholesky.148 = f32[128,128]{1,0:T(8,128)S(1)} custom-call(f32[128,128]{1,0:T(8,128)S(1)} %fusion.79), custom_call_target="Cholesky" | custom-call | tf_op jit(solution)/shard_map/jit(cholesky)/cholesky | solution.py:28
  310.4 10.0 %custom-call.14 = f32[1,128,128]{1,2,0:T(8,128)S(1)} custom-call(f32[1,128,128]{2,1,0:T(8,128)S(1)} %get-tuple-element.52), custom_call_target="InvertDiagBlocksLowerTriangular" | custom-call | tf_op jit(solution)/shard_map/triangular_solve/custom-call.0 | solution.py:29
  321.3 11.7 %cholesky.159 = f32[128,128]{1,0:T(8,128)S(1)} custom-call(f32[128,128]{1,0:T(8,128)S(1)} %fusion.77), custom_call_target="Cholesky" | custom-call | tf_op jit(solution)/shard_map/jit(cholesky)/cholesky | solution.py:31
  334.4 9.8 %custom-call.15 = f32[1,128,128]{1,2,0:T(8,128)S(1)} custom-call(f32[1,128,128]{2,1,0:T(8,128)S(1)} %get-tuple-element.50), custom_call_target="InvertDiagBlocksLowerTriangular" | custom-call | tf_op jit(solution)/shard_map/triangular_solve/custom-call.0 | solution.py:32
  349.8 9.1 %fusion.140 = (f32[1,4096,256]{2,1,0:T(8,128)}, f32[1,4096,256]{2,1,0:T(8,128)S(1)}, f32[1,4096,256]{2,1,0:T(8,128)}) fusion(f32[3,4096,256]{2,1,0:T(8,128)} %all-gather.11.cloned.1.call-done), kind=kLoop, calls=%fused_computation.219 | loop fusion | bytes 25165824 | tf_op jit(solution)/shard_map/slice | solution.py:102
  358.9 5.7 %fusion.36 = f32[16,256,256]{2,1,0:T(8,128)S(1)} fusion(f32[16,256,256]{2,1,0:T(8,128)} %bitcast.216, f32[128,128]{1,0:T(8,128)S(1)} %fusion.51, f32[128,128]{1,0:T(8,128)S(1)} %copy.86, f32[128,128]{1,0:T(8,128)S(1)} %convolution_negate_fusion.2), kind=kOutput, calls=%fused_computation.78 | convolution fusion | flops 3221487616 | bytes 8585216 | tf_op jit(solution)/shard_map/...ps,qs->...pq/dot_general | solution.py:11
  366.5 3.7 fusion.6
  373.7 6.1 %fusion.3 = f32[16,256,256]{2,1,0:T(8,128)S(1)} fusion(f32[16,256,256]{2,1,0:T(8,128)S(1)} %fusion.15, f32[16,256,256]{2,1,0:T(8,128)} %bitcast.217, f32[16,256,256]{2,1,0:T(8,128)S(1)} %fusion.17, f32[128,128]{1,0:T(8,128)S(1)} %fusion.43, f32[128,128]{1,0:T(8,128)S(1)} %copy.101, f32[128,128]{1,0:T(8,128)S(1)} %convolution_negate_fusion), kind=kOutput, calls=%fused_computation.5 | convolution fusion | flops 3223584768 | bytes 16973824 | tf_op jit(solution)/shard_map/...ps,qs->...pq/dot_general | solution.py:11
  381.7 3.7 fusion.1
  385.5 6.3 %copy.105 = f32[16,1,256,1,1,256]{5,4,3,2,1,0:T(1,128)} copy(f32[16,1,256,1,1,256]{5,2,0,4,3,1:T(8,128)S(1)} %fusion.1) | data formatting | bytes 8388608 | tf_op jit(solution)/shard_map/reshape | solution.py:137
  (123 shorter events, 36.1 us)
Async XLA Ops:
  6.5 31.2 %all-gather.7.cloned.1.call-start = ((), (), s32[]{:S(2)}) async-start(), calls=%async_computation.1 | async-start | bytes 1310720 | tf_op jit(solution)/shard_map/all_gather | solution.py:51
  8.4 139.9 %all-gather.9.cloned.1.call-start = ((), (), s32[]{:S(2)}) async-start(), calls=%async_computation.2 | async-start | bytes 2396160 | tf_op jit(solution)/shard_map/all_gather | solution.py:57
  73.4 276.4 %all-gather.11.cloned.1.call-start = ((), (), s32[]{:S(2)}) async-start(), calls=%async_computation.3 | async-start | bytes 12779520 | tf_op jit(solution)/shard_map/all_gather | solution.py:69
  73.8 74.5 %copy-start = (f32[3,1,256,1,1,256]{2,5,0,4,3,1:T(8,128)}, f32[3,1,256,1,1,256]{2,5,0,4,3,1:T(8,128)S(1)}, u32[]{:S(2)}) copy-start(f32[3,1,256,1,1,256]{2,5,0,4,3,1:T(8,128)S(1)} %copy.118) | copy-start | bytes 2359300
  159.9 11.2 %collective-permute-start = (f32[3,64,256]{2,1,0:T(8,128)S(1)}, f32[3,64,256]{2,1,0:T(8,128)S(1)}, u32[]{:S(2)}, u32[]{:S(2)}) collective-permute-start(f32[3,64,256]{2,1,0:T(8,128)S(1)} %dynamic-slice_bitcast_fusion), channel_id=1, source_target_pairs={{0,0},{1,4},{2,8},{3,12},{4,1},{5,5},{6,9},{7,13},{8,2},{9,6},{10,... | collective-permute-start | bytes 589832 | tf_op jit(solution)/shard_map/ppermute | solution.py:67
  171.2 0.7 copy-start.6
  179.7 59.4 %copy-start.3 = (f32[64,3072]{1,0:T(8,128)S(1)}, f32[64,3072]{1,0:T(8,128)}, u32[]{:S(2)}) copy-start(f32[64,3072]{1,0:T(8,128)} %get-tuple-element.47) | copy-start | bytes 2359300
  179.7 62.4 %copy-start.2 = (f32[64,3072]{1,0:T(8,128)S(1)}, f32[64,3072]{1,0:T(8,128)}, u32[]{:S(2)}) copy-start(f32[64,3072]{1,0:T(8,128)} %get-tuple-element.48) | copy-start | bytes 2359300
  293.8 52.4 %copy-start.1 = (f32[3,1,256,1,1,256]{2,5,0,4,3,1:T(8,128)S(1)}, f32[3,1,256,1,1,256]{2,5,0,4,3,1:T(8,128)}, u32[]{:S(2)}) copy-start(f32[3,1,256,1,1,256]{2,5,0,4,3,1:T(8,128)} %copy-done) | copy-start | bytes 2359300
  294.5 50.1 %copy-start.4 = (f32[128,128]{1,0:T(8,128)S(1)}, f32[128,128]{1,0:T(8,128)}, u32[]{:S(2)}) copy-start(f32[128,128]{1,0:T(8,128)} %get-tuple-element.55) | copy-start | bytes 196612
  295.3 49.2 %copy-start.5 = (f32[128,128]{1,0:T(8,128)S(1)}, f32[128,128]{1,0:T(8,128)}, u32[]{:S(2)}) copy-start(f32[128,128]{1,0:T(8,128)} %copy.103) | copy-start | bytes 196612
Sparse Core Ops, SparseCore 0:
  9.1 28.5 all-gather.6
  73.6 74.6 all-gather.8
  172.0 87.4 all-gather.10
